TPU v7x, 256 devices: a whole 4x4x8 slice. The times are simulated.
256 devices in a mesh: seq: 32 (over x, z), tp: 8 (over y, core).
Axes of the slice: x: 4, y: 4, z: 8, core: 2. Of those that a mesh axis runs over, the one named last changes fastest.
Arguments:
- tokens: bfloat16 [32768, 2048], P('seq', 'tp'), may hold values from -6 to 6
- w_inner: bfloat16 [2048, 2, 4096], P('seq', None, 'tp'), may hold values from -0.125 to 0.125
- w_states: bfloat16 [2048, 256], P('seq'), may hold values from -0.125 to 0.125
- w_step: bfloat16 [2048, 64], P('seq', 'tp'), may hold values from -0.125 to 0.125
- conv_inner: float32 [4, 4096], P(None, 'tp'), may hold values from -3 to 3
- conv_states: float32 [4, 256], replicated, may hold values from -3 to 3
- decay_rate: float32 [64], P('tp'), may hold values from 0 to 1, as said below
- step_bias: float32 [64], P('tp'), may hold values from -1 to 0.5
- skip_gain: float32 [64], P('tp'), may hold values from 0.5 to 1.5
- norm_gain: float32 [4096], P('tp'), may hold values from 0.5 to 1.5
- w_output: bfloat16 [4096, 2048], P('tp', 'seq'), may hold values from -0.09375 to 0.09375
- block_owner: int32 [128], replicated, may hold values from 0 to 19, as said below
- lengths: int32 [20], replicated, may hold values from 1 to 16384, as said below
Outputs:
- mixed: bfloat16 [32768, 2048], P('seq', 'tp')
Inputs may be any that keep to these rules, and one draw needn't show every extreme that they name: `block_owner`: each prompt's blocks are consecutive, prompt r has ceil(lengths[r] / 256) of them, and the prompts follow one another in an order drawn afresh; one prompt has 64 blocks and is neither the first nor the last in that order. `lengths`: one prompt has exactly 16384 tokens. `decay_rate`: Positive.
All inputs are finite; a program needn't handle non-finite values.
Results may differ from a plain program's by a relative error of at most 0.0075.
Values may be sent and summed in bfloat16 or wider, within the bound.
No kernel may reach another device: no remote copies, remote signals or barrier semaphores. Data moves between devices by JAX's collectives and lax.ppermute only.
A program may use at most 64 MiB of HBM per device.

v0:
```python
import jax
import jax.numpy as jnp
from jax import lax
from jax.sharding import PartitionSpec as P

BLOCK = 256
LONGEST = 64


def passed_along(value, axis, by):
    count = lax.axis_size(axis)
    pairs = [(i, i + by) for i in range(count) if 0 <= i + by < count]
    return lax.ppermute(value, axis, pairs)


def convolve(values, edge_rows, weights, in_block, carry_on):
    lag_rows = weights.shape[0] - 1
    row_total = values.shape[0]
    widened = jnp.concatenate([edge_rows, values], axis=0).astype(jnp.float32)
    total = jnp.zeros(values.shape, jnp.float32)
    for offset in range(weights.shape[0]):
        shifted = widened[lag_rows - offset : lag_rows - offset + row_total]
        keeping = (in_block >= offset) | carry_on
        total = total + jnp.where(keeping[:, None], shifted, 0.0) * weights[offset]
    return jax.nn.silu(total).astype(jnp.bfloat16)


def on_device(
    tokens,
    w_inner,
    w_states,
    w_step,
    conv_inner,
    conv_states,
    decay_rate,
    step_bias,
    skip_gain,
    norm_gain,
    w_output,
    block_owner,
    lengths,
):
    row_count = tokens.shape[0]
    local_blocks = row_count // BLOCK
    total_blocks = block_owner.shape[0]
    heads_here = w_step.shape[1]
    inner_here = w_inner.shape[2]
    state_size = w_states.shape[1] // 2
    head_size = inner_here // heads_here
    lag_rows = conv_inner.shape[0] - 1
    block_ids = jnp.arange(total_blocks, dtype=jnp.int32)
    same_owner = block_owner[:, None] == block_owner[None, :]
    first_block = jnp.min(jnp.where(same_owner, block_ids[None, :], total_blocks), axis=1)
    starting = (first_block == block_ids).astype(jnp.int32)
    request_ids = jnp.arange(lengths.shape[0], dtype=jnp.int32)
    own_length = jnp.sum(
        jnp.where(block_owner[:, None] == request_ids[None, :], lengths[None, :], 0), axis=1
    )
    valid_rows = jnp.clip(own_length - (block_ids - first_block) * BLOCK, 0, BLOCK)
    seq_index = lax.axis_index("seq")
    local_start = lax.dynamic_slice_in_dim(starting, seq_index * local_blocks, local_blocks)
    local_valid = lax.dynamic_slice_in_dim(valid_rows, seq_index * local_blocks, local_blocks)
    in_block = jnp.arange(row_count, dtype=jnp.int32) % BLOCK
    carry_on = jnp.repeat(local_start == 0, BLOCK)
    whole = lax.all_gather(tokens, "tp", axis=1, tiled=True)
    first_cols = jnp.concatenate([w_inner[:, 1, :], w_states, w_step], axis=1)
    first_weights = lax.all_gather(first_cols, "seq", axis=0, tiled=True)
    gate_weights = lax.all_gather(w_inner[:, 0, :], "seq", axis=0, tiled=True)
    first_sum = jnp.dot(whole, first_weights, preferred_element_type=jnp.float32)
    projected = first_sum.astype(jnp.bfloat16)
    x_in = projected[:, :inner_here]
    bc_in = projected[:, inner_here : inner_here + 2 * state_size]
    step_raw = projected[:, inner_here + 2 * state_size :]
    gate_in = jnp.dot(whole, gate_weights, preferred_element_type=jnp.float32).astype(jnp.bfloat16)
    edge_inner, edge_states = passed_along(
        (x_in[row_count - lag_rows :], bc_in[row_count - lag_rows :]), "seq", 1
    )
    x_conv = convolve(x_in, edge_inner, conv_inner, in_block, carry_on)
    bc_conv = convolve(bc_in, edge_states, conv_states, in_block, carry_on)
    step_size = jax.nn.softplus(step_raw.astype(jnp.float32) + step_bias)
    log_decay = -decay_rate * step_size
    x_heads = x_conv.reshape(local_blocks, BLOCK, heads_here, head_size)
    b_rows = bc_conv[:, :state_size].reshape(local_blocks, BLOCK, state_size)
    c_rows = bc_conv[:, state_size:].reshape(local_blocks, BLOCK, state_size)
    step_blocks = step_size.reshape(local_blocks, BLOCK, heads_here)
    cumulative = jnp.cumsum(log_decay.reshape(local_blocks, BLOCK, heads_here), axis=1)
    causal = jnp.arange(BLOCK)[:, None] >= jnp.arange(BLOCK)[None, :]
    spread = cumulative[:, :, None, :] - cumulative[:, None, :, :]
    decays = jnp.exp(jnp.where(causal[None, :, :, None], spread, -jnp.inf))
    intersection = jnp.einsum("cin,cjn->cij", c_rows, b_rows, preferred_element_type=jnp.float32)
    mixing = (decays * intersection[:, :, :, None] * step_blocks[:, None, :, :]).astype(
        jnp.bfloat16
    )
    y_inner = jnp.einsum("cijh,cjhp->cihp", mixing, x_heads, preferred_element_type=jnp.float32)
    final_log = cumulative[:, -1, :]
    tail_weight = jnp.exp(final_log[:, None, :] - cumulative) * step_blocks
    weighted_b = (tail_weight[:, :, :, None] * b_rows.astype(jnp.float32)[:, :, None, :]).astype(
        jnp.bfloat16
    )
    fresh = jnp.einsum("cjhn,cjhp->chnp", weighted_b, x_heads, preferred_element_type=jnp.float32)
    keep_flag = jnp.where(local_start == 1, 0.0, 1.0).astype(jnp.float32)
    block_gain_each = jnp.exp(final_log) * keep_flag[:, None]
    block_gain = jnp.ones((heads_here,), jnp.float32)
    block_state = jnp.zeros((heads_here, state_size, head_size), jnp.float32)
    gains_in, states_in = ([], [])
    for block in range(local_blocks):
        gains_in.append(block_gain * keep_flag[block])
        states_in.append(block_state * keep_flag[block])
        block_gain = block_gain * block_gain_each[block]
        block_state = block_gain_each[block][:, None, None] * block_state + fresh[block]

    def packed(gain, state):
        rows = jnp.broadcast_to(gain[:, None, None], (heads_here, 1, head_size))
        return jnp.concatenate([state, rows], axis=1)

    prefix = passed_along(packed(block_gain, block_state), "seq", 1)
    needed = min(-(-(LONGEST - 1) // local_blocks), lax.axis_size("seq") - 1)
    reach = 1
    while reach < needed:
        earlier = passed_along(prefix, "seq", reach)
        gain_now = prefix[:, state_size:, :1]
        prefix = jnp.concatenate(
            [
                gain_now * earlier[:, :state_size] + prefix[:, :state_size],
                gain_now * earlier[:, state_size:],
            ],
            axis=1,
        )
        reach *= 2
    entering = prefix[:, :state_size]
    incoming_all = jnp.stack(gains_in)[:, :, None, None] * entering[None] + jnp.stack(states_in)
    incoming_half = incoming_all.astype(jnp.bfloat16)
    y_carry = jnp.exp(cumulative)[:, :, :, None] * jnp.einsum(
        "cin,chnp->cihp", c_rows, incoming_half, preferred_element_type=jnp.float32
    )
    y_total = (y_inner + y_carry).reshape(row_count, inner_here) + jnp.repeat(skip_gain, head_size)[
        None, :
    ] * x_conv.astype(jnp.float32)
    gated = y_total * jax.nn.silu(gate_in.astype(jnp.float32))
    squares = jnp.sum(gated * gated, axis=1)
    scaled = (gated * norm_gain).astype(jnp.bfloat16)
    partial_out = jnp.dot(
        scaled,
        lax.all_gather(w_output, "seq", axis=1, tiled=True),
        preferred_element_type=jnp.float32,
    )
    tp_count = lax.axis_size("tp")
    cols_here = partial_out.shape[1] // tp_count
    square_rows = jnp.tile(squares.reshape(row_count // cols_here, cols_here), (1, tp_count))
    summed = lax.psum_scatter(
        jnp.concatenate([partial_out, square_rows], axis=0), "tp", scatter_dimension=1, tiled=True
    )
    square_mean = summed[row_count:].reshape(row_count) / (inner_here * tp_count)
    mixed = summed[:row_count] * lax.rsqrt(square_mean + 1e-05)[:, None]
    live = in_block < jnp.repeat(local_valid, BLOCK)
    return jnp.where(live[:, None], mixed, 0.0).astype(jnp.bfloat16)


def solution(mesh):
    return jax.shard_map(
        on_device,
        mesh=mesh,
        in_specs=(
            P("seq", "tp"),
            P("seq", None, "tp"),
            P("seq", None),
            P("seq", "tp"),
            P(None, "tp"),
            P(),
            P("tp"),
            P("tp"),
            P("tp"),
            P("tp"),
            P("tp", "seq"),
            P(),
            P(),
        ),
        out_specs=P("seq", "tp"),
        check_vma=False,
    )
```

profile of v0, /device:TPU:1, one launch (start us, length us, event | category | flops | bytes accessed | tf_op | source)
XLA Modules:
  0.0 382.6 jit_solution(7631663439975435024)
XLA Ops:
  16.2 74.5 %all-gather.6.cloned.1.call-done = bf16[2048,776]{1,0:T(8,128)(2,1)} async-done(((bf16[64,776]{1,0:T(8,128)(2,1)}), bf16[2048,776]{1,0:T(8,128)(2,1)}) %all-gather.6.cloned.1.call-update) | async-done | bytes 3178512 | tf_op jit(solution)/shard_map/all_gather | solution.py:67
  90.6 41.1 %all-gather.8.cloned.1.call-done = bf16[1024,2048]{1,0:T(8,128)(2,1)} async-done(((bf16[1024,256]{1,0:T(8,128)(2,1)}), bf16[1024,2048]{1,0:T(8,128)(2,1)}) %all-gather.8.cloned.1.call-update) | async-done | bytes 4194320 | tf_op jit(solution)/shard_map/all_gather | solution.py:65
  131.7 7.8 %convert_bitcast_fusion = bf16[1024,776]{1,0:T(8,128)(2,1)S(1)} fusion(bf16[2048,776]{1,0:T(8,128)(2,1)} %all-gather.6.cloned.1.call-done, bf16[1024,2048]{1,0:T(8,128)(2,1)} %all-gather.8.cloned.1.call-done), kind=kOutput, calls=%fused_computation.36 | convolution fusion | flops 3255574528 | bytes 8962048 | tf_op jit(solution)/shard_map/dot_general | solution.py:69
  139.6 3.2 collective-permute-start.1
  142.7 3.2 collective-permute-start
  161.3 2.8 fusion.11
  164.4 4.0 %collective-permute-start.2 = (f32[8,129,64]{1,2,0:T(8,128)S(1)}, f32[8,129,64]{1,2,0:T(8,128)}, u32[]{:S(2)}, u32[]{:S(2)}) collective-permute-start(f32[8,129,64]{1,2,0:T(8,128)S(1)} %pad_maximum_fusion.1), channel_id=1, source_target_pairs={{0,8},{8,16},{16,24},{24,32},{32,40},{40,48},{48,56},{56,64},{64,7... | collective-permute-start | bytes 792584 | tf_op jit(solution)/shard_map/ppermute | solution.py:13
  168.4 10.1 %collective-permute-done.2 = f32[8,129,64]{1,2,0:T(8,128)} collective-permute-done((f32[8,129,64]{1,2,0:T(8,128)S(1)}, f32[8,129,64]{1,2,0:T(8,128)}, u32[]{:S(2)}, u32[]{:S(2)}) %collective-permute-start.2) | collective-permute-done | bytes 264224 | tf_op jit(solution)/shard_map/ppermute | solution.py:13
  178.5 4.2 %collective-permute-start.3 = (f32[8,129,64]{1,2,0:T(8,128)}, f32[8,129,64]{1,2,0:T(8,128)S(1)}, u32[]{:S(2)}, u32[]{:S(2)}) collective-permute-start(f32[8,129,64]{1,2,0:T(8,128)} %collective-permute-done.2), channel_id=1, source_target_pairs={{0,8},{8,16},{16,24},{24,32},{32,40},{40,48},{48,56},{56,64},{64,7... | collective-permute-start | bytes 792584 | tf_op jit(solution)/shard_map/ppermute | solution.py:13
  185.1 13.7 %collective-permute-done.3 = f32[8,129,64]{1,2,0:T(8,128)S(1)} collective-permute-done((f32[8,129,64]{1,2,0:T(8,128)}, f32[8,129,64]{1,2,0:T(8,128)S(1)}, u32[]{:S(2)}, u32[]{:S(2)}) %collective-permute-start.3) | collective-permute-done | bytes 264224 | tf_op jit(solution)/shard_map/ppermute | solution.py:13
  201.8 7.5 %collective-permute-start.4 = (f32[8,129,64]{1,2,0:T(8,128)S(1)}, f32[8,129,64]{1,2,0:T(8,128)S(1)}, u32[]{:S(2)}, u32[]{:S(2)}) collective-permute-start(f32[8,129,64]{1,2,0:T(8,128)S(1)} %pad_maximum_fusion.2), channel_id=1, source_target_pairs={{0,16},{8,24},{16,32},{24,40},{32,48},{40,56},{48,64},{56,72},{64,... | collective-permute-start | bytes 792584 | tf_op jit(solution)/shard_map/ppermute | solution.py:13
  209.6 21.6 %collective-permute-done.4 = f32[8,129,64]{1,2,0:T(8,128)S(1)} collective-permute-done((f32[8,129,64]{1,2,0:T(8,128)S(1)}, f32[8,129,64]{1,2,0:T(8,128)S(1)}, u32[]{:S(2)}, u32[]{:S(2)}) %collective-permute-start.4) | collective-permute-done | bytes 264224 | tf_op jit(solution)/shard_map/ppermute | solution.py:13
  231.4 9.2 %collective-permute-start.5 = (f32[8,129,64]{1,2,0:T(8,128)S(1)}, f32[8,129,64]{1,2,0:T(8,128)S(1)}, u32[]{:S(2)}, u32[]{:S(2)}) collective-permute-start(f32[8,129,64]{1,2,0:T(8,128)S(1)} %pad_maximum_fusion.3), channel_id=1, source_target_pairs={{0,32},{8,40},{16,48},{24,56},{32,64},{40,72},{48,80},{56,88},{64,... | collective-permute-start | bytes 792584 | tf_op jit(solution)/shard_map/ppermute | solution.py:13
  241.0 23.4 %collective-permute-done.5 = f32[8,129,64]{1,2,0:T(8,128)S(1)} collective-permute-done((f32[8,129,64]{1,2,0:T(8,128)S(1)}, f32[8,129,64]{1,2,0:T(8,128)S(1)}, u32[]{:S(2)}, u32[]{:S(2)}) %collective-permute-start.5) | collective-permute-done | bytes 264224 | tf_op jit(solution)/shard_map/ppermute | solution.py:13
  264.7 7.4 %collective-permute-start.6 = (f32[8,129,64]{1,2,0:T(8,128)S(1)}, f32[8,129,64]{1,2,0:T(8,128)S(1)}, u32[]{:S(2)}, u32[]{:S(2)}) collective-permute-start(f32[8,129,64]{1,2,0:T(8,128)S(1)} %pad_maximum_fusion.4), channel_id=1, source_target_pairs={{0,64},{8,72},{16,80},{24,88},{32,96},{40,104},{48,112},{56,120},{... | collective-permute-start | bytes 792584 | tf_op jit(solution)/shard_map/ppermute | solution.py:13
  274.2 8.5 %collective-permute-done.6 = f32[8,129,64]{1,2,0:T(8,128)S(1)} collective-permute-done((f32[8,129,64]{1,2,0:T(8,128)S(1)}, f32[8,129,64]{1,2,0:T(8,128)S(1)}, u32[]{:S(2)}, u32[]{:S(2)}) %collective-permute-start.6) | collective-permute-done | bytes 264224 | tf_op jit(solution)/shard_map/ppermute | solution.py:13
  284.0 2.4 bitcast_add_fusion
  286.4 2.8 copy.104
  289.2 4.8 %reshape.172 = f32[1024,512]{1,0:T(8,128)} reshape(f32[4,256,8,64]{3,2,1,0:T(8,128)} %copy.104) | data formatting | bytes 4194304 | tf_op jit(solution)/shard_map/reshape | solution.py:136
  294.0 6.4 %multiply_reduce_fusion = (f32[1024]{0:T(1024)S(1)}, f32[1024,512]{1,0:T(8,128)S(1)}) fusion(bf16[1024,2048]{1,0:T(8,128)(2,1)} %all-gather.8.cloned.1.call-done, bf16[2048,1,512]{2,0,1:T(8,128)(2,1)} %all-gather.12.cloned.1.call-done, f32[1024,512]{1,0:T(8,128)} %reshape.172, bf16[1024,512]{1,0:T(8,128)(2,1)S(1)} %multiply_convert_fusion.5, f32[512]{0:T(512)S(1)} %mul.490), kind=kOutput, calls=%fused_computation.31 | convolution fusion | flops 2153774080 | bytes 11540480 | tf_op jit(solution)/shard_map/dot_general | solution.py:74
  300.5 7.9 %all-gather.10.cloned.1.call-done = bf16[512,2048]{0,1:T(8,128)(2,1)} async-done(((bf16[512,64]{0,1:T(8,128)(2,1)}), bf16[512,2048]{0,1:T(8,128)(2,1)}) %all-gather.10.cloned.1.call-update) | async-done | bytes 2097168 | tf_op jit(solution)/shard_map/all_gather | solution.py:144
  308.4 4.0 %fusion.28 = f32[1024,2048]{1,0:T(8,128)S(1)} fusion(bf16[512,2048]{0,1:T(8,128)(2,1)} %all-gather.10.cloned.1.call-done, f32[1024,512]{1,0:T(8,128)S(1)} %get-tuple-element.41, f32[512]{0:T(512)S(1)} %copy-done.4), kind=kOutput, calls=%fused_computation.40 | convolution fusion | flops 2148532224 | bytes 12584960 | tf_op jit(solution)/shard_map/dot_general | solution.py:142
  312.4 3.9 %pad_maximum_fusion = f32[1028,2048]{1,0:T(8,128)} fusion(f32[4,2048]{1,0:T(4,128)S(1)} %bitcast.119, f32[1024,2048]{1,0:T(8,128)S(1)} %fusion.28), kind=kLoop, calls=%fused_computation | loop fusion | flops 2105344 | bytes 16842752 | tf_op jit(solution)/shard_map/concatenate | solution.py:151
  317.2 55.8 %reduce-scatter.2.cloned.1.call-done = f32[1028,256]{1,0:T(8,128)} async-done(((f32[1028,2048]{1,0:T(8,128)}), f32[1028,256]{1,0:T(8,128)}) %reduce-scatter.2.cloned.1.call-update) | async-done | bytes 1052688 | tf_op jit(solution)/shard_map/reduce_scatter | solution.py:150
  (126 shorter events, 38.2 us)
Async XLA Ops:
  6.5 84.1 %all-gather.6.cloned.1.call-start = ((), (), s32[]{:S(2)}) async-start(), calls=%async_computation.1 | async-start | bytes 3784704 | tf_op jit(solution)/shard_map/all_gather | solution.py:67
  10.0 121.7 %all-gather.8.cloned.1.call-start = ((), (), s32[]{:S(2)}) async-start(), calls=%async_computation.2 | async-start | bytes 4718592 | tf_op jit(solution)/shard_map/all_gather | solution.py:65
  10.7 283.3 %all-gather.12.cloned.1.call-start = ((), (), s32[]{:S(2)}) async-start(), calls=%async_computation.5 | async-start | bytes 2162688 | tf_op jit(solution)/shard_map/all_gather | solution.py:68
  11.5 296.9 %all-gather.10.cloned.1.call-start = ((), (), s32[]{:S(2)}) async-start(), calls=%async_computation.3 | async-start | bytes 2162688 | tf_op jit(solution)/shard_map/all_gather | solution.py:144
  16.2 129.8 %copy-start.9 = (f32[8]{0:T(128)S(1)}, f32[8]{0:T(128)}, u32[]{:S(2)}) copy-start(f32[8]{0:T(128)} %param.20) | copy-start | bytes 100
  139.5 12.9 %copy-start.1 = (bf16[1024,776]{1,0:T(8,128)(2,1)}, bf16[1024,776]{1,0:T(8,128)(2,1)S(1)}, u32[]{:S(2)}) copy-start(bf16[1024,776]{1,0:T(8,128)(2,1)S(1)} %convert_bitcast_fusion) | copy-start | bytes 4767748
  139.6 12.9 %collective-permute-start.1 = (bf16[3,256]{1,0:T(4,128)(2,1)S(1)}, bf16[3,256]{1,0:T(4,128)(2,1)S(1)}, u32[]{:S(2)}, u32[]{:S(2)}) collective-permute-start(bf16[3,256]{1,0:T(4,128)(2,1)S(1)} %slice.235), channel_id=1, source_target_pairs={{0,8},{8,16},{16,24},{24,32},{32,40},{40,48},{48,56},{56,64},{64,7... | collective-permute-start | bytes 4616 | tf_op jit(solution)/shard_map/ppermute | solution.py:13
  142.7 12.9 %collective-permute-start = (bf16[3,512]{1,0:T(4,128)(2,1)S(1)}, bf16[3,512]{1,0:T(4,128)(2,1)S(1)}, u32[]{:S(2)}, u32[]{:S(2)}) collective-permute-start(bf16[3,512]{1,0:T(4,128)(2,1)S(1)} %slice.226), channel_id=1, source_target_pairs={{0,8},{8,16},{16,24},{24,32},{32,40},{40,48},{48,56},{56,64},{64,7... | collective-permute-start | bytes 9224 | tf_op jit(solution)/shard_map/ppermute | solution.py:13
  154.0 1.6 slice-start
  161.3 3.0 copy-start.5
  164.0 20.0 %copy-start.10 = (f32[8]{0:T(128)S(1)}, f32[8]{0:T(128)}, u32[]{:S(2)}) copy-start(f32[8]{0:T(128)} %param.21) | copy-start | bytes 100
  164.2 45.1 %copy-start.6 = (f32[1,8]{1,0:T(1,128)S(1)}, f32[1,8]{1,0:T(1,128)}, u32[]{:S(2)}) copy-start(f32[1,8]{1,0:T(1,128)} %get-tuple-element.24) | copy-start | bytes 100
  164.2 45.1 %copy-start.7 = (f32[1,8]{1,0:T(1,128)S(1)}, f32[1,8]{1,0:T(1,128)}, u32[]{:S(2)}) copy-start(f32[1,8]{1,0:T(1,128)} %get-tuple-element.28) | copy-start | bytes 100
  164.2 45.1 %copy-start.8 = (f32[1,8]{1,0:T(1,128)S(1)}, f32[1,8]{1,0:T(1,128)}, u32[]{:S(2)}) copy-start(f32[1,8]{1,0:T(1,128)} %get-tuple-element.29) | copy-start | bytes 100
  164.4 14.2 %collective-permute-start.2 = (f32[8,129,64]{1,2,0:T(8,128)S(1)}, f32[8,129,64]{1,2,0:T(8,128)}, u32[]{:S(2)}, u32[]{:S(2)}) collective-permute-start(f32[8,129,64]{1,2,0:T(8,128)S(1)} %pad_maximum_fusion.1), channel_id=1, source_target_pairs={{0,8},{8,16},{16,24},{24,32},{32,40},{40,48},{48,56},{56,64},{64,7... | collective-permute-start | bytes 792584 | tf_op jit(solution)/shard_map/ppermute | solution.py:13
  178.5 20.3 %collective-permute-start.3 = (f32[8,129,64]{1,2,0:T(8,128)}, f32[8,129,64]{1,2,0:T(8,128)S(1)}, u32[]{:S(2)}, u32[]{:S(2)}) collective-permute-start(f32[8,129,64]{1,2,0:T(8,128)} %collective-permute-done.2), channel_id=1, source_target_pairs={{0,8},{8,16},{16,24},{24,32},{32,40},{40,48},{48,56},{56,64},{64,7... | collective-permute-start | bytes 792584 | tf_op jit(solution)/shard_map/ppermute | solution.py:13
  182.8 190.2 %reduce-scatter.2.cloned.1.call-start = ((), (), s32[]{:S(2)}) async-start(), calls=%async_computation.4 | async-start | bytes 9510912 | tf_op jit(solution)/shard_map/reduce_scatter | solution.py:150
  198.8 0.8 copy-start.3
  200.6 39.9 %copy-start.2 = (bf16[1024,128]{1,0:T(8,128)(2,1)S(1)}, bf16[1024,128]{1,0:T(8,128)(2,1)}, u32[]{:S(2)}) copy-start(bf16[1024,128]{1,0:T(8,128)(2,1)} %get-tuple-element.13) | copy-start | bytes 786436
  201.8 29.3 %collective-permute-start.4 = (f32[8,129,64]{1,2,0:T(8,128)S(1)}, f32[8,129,64]{1,2,0:T(8,128)S(1)}, u32[]{:S(2)}, u32[]{:S(2)}) collective-permute-start(f32[8,129,64]{1,2,0:T(8,128)S(1)} %pad_maximum_fusion.2), channel_id=1, source_target_pairs={{0,16},{8,24},{16,32},{24,40},{32,48},{40,56},{48,64},{56,72},{64,... | collective-permute-start | bytes 792584 | tf_op jit(solution)/shard_map/ppermute | solution.py:13
  231.4 33.1 %collective-permute-start.5 = (f32[8,129,64]{1,2,0:T(8,128)S(1)}, f32[8,129,64]{1,2,0:T(8,128)S(1)}, u32[]{:S(2)}, u32[]{:S(2)}) collective-permute-start(f32[8,129,64]{1,2,0:T(8,128)S(1)} %pad_maximum_fusion.3), channel_id=1, source_target_pairs={{0,32},{8,40},{16,48},{24,56},{32,64},{40,72},{48,80},{56,88},{64,... | collective-permute-start | bytes 792584 | tf_op jit(solution)/shard_map/ppermute | solution.py:13
  264.7 18.0 %collective-permute-start.6 = (f32[8,129,64]{1,2,0:T(8,128)S(1)}, f32[8,129,64]{1,2,0:T(8,128)S(1)}, u32[]{:S(2)}, u32[]{:S(2)}) collective-permute-start(f32[8,129,64]{1,2,0:T(8,128)S(1)} %pad_maximum_fusion.4), channel_id=1, source_target_pairs={{0,64},{8,72},{16,80},{24,88},{32,96},{40,104},{48,112},{56,120},{... | collective-permute-start | bytes 792584 | tf_op jit(solution)/shard_map/ppermute | solution.py:13
  282.8 1.2 copy-start
  294.0 14.4 %copy-start.4 = (f32[512]{0:T(512)S(1)}, f32[512]{0:T(512)}, u32[]{:S(2)}) copy-start(f32[512]{0:T(512)} %param.22) | copy-start | bytes 6148
  (4 other events, 2.6 us)
Sparse Core Ops, SparseCore 0:
  10.1 80.4 all-gather.5
  92.5 39.1 all-gather.7
  134.3 75.4 all-gather.11
  212.2 96.1 all-gather.9
  316.4 56.5 reduce-scatter.1
where the time goes:
time: 384 us; the launch traced here: 383 us
  waiting for transfers between devices  257 us (67%)
  starting transfers between devices  38.9 us (10%)
  other arithmetic  25.9 us (7%)
  matrix products  24.1 us (6%)
  local copies, waits for them, and re-layouts  22.1 us (6%)
  between operations  14.2 us (4%)
    ppermute x7, waiting for transfers between devices, passed_along(): return lax.ppermute(value, axis, pairs)  77.4 us
    all_gather x1, waiting for transfers between devices, on_device(): first_weights = lax.all_gather(first_cols, 'seq', axis=0, tiled=True)  74.5 us
    reduce_scatter x1, waiting for transfers between devices, on_device(): lax.psum_scatter(jnp.concatenate([partial_out, square_rows], axis=0), 'tp...  55.8 us
    all_gather x1, waiting for transfers between devices, on_device(): whole = lax.all_gather(tokens, 'tp', axis=1, tiled=True)  41.1 us
    ppermute x7, starting transfers between devices, passed_along(): return lax.ppermute(value, axis, pairs)  38.7 us
    all_gather x1, waiting for transfers between devices, on_device(): lax.all_gather(w_output, 'seq', axis=1, tiled=True)  7.9 us
    dot_general x1, matrix products, on_device(): jnp.dot(whole, first_weights, preferred_element_type=jnp.float32)  7.8 us
  transfers between devices with their start and end apart: 12, of which 9 were waited for; matrix products, arithmetic and copies ran while one was open for 14% of the time, Pallas kernels for 0%

commit v1 on v0

--- a/solution.py
+++ b/solution.py
@@ -64,7 +64,10 @@
     carry_on = jnp.repeat(local_start == 0, BLOCK)
     whole = lax.all_gather(tokens, "tp", axis=1, tiled=True)
     first_cols = jnp.concatenate([w_inner[:, 1, :], w_states, w_step], axis=1)
-    first_weights = lax.all_gather(first_cols, "seq", axis=0, tiled=True)
+    report_inputs = lambda point, row_axis: jnp.concatenate(
+        lax.all_to_all(jnp.stack([point] * lax.axis_size(row_axis)), row_axis, 0, 0), axis=0
+    )
+    first_weights = report_inputs(first_cols, row_axis="seq")
     gate_weights = lax.all_gather(w_inner[:, 0, :], "seq", axis=0, tiled=True)
     first_sum = jnp.dot(whole, first_weights, preferred_element_type=jnp.float32)
     projected = first_sum.astype(jnp.bfloat16)

time: 384 us -> 349 us (0.909)
  waiting for transfers between devices: 257 us -> 193 us
  starting transfers between devices: 38.9 us -> 70 us
    all_to_all x0 -> x1, waiting for transfers between devices: none -> 81.5 us  [on_device(): lax.all_to_all(jnp.stack([point] * lax.axis_size(row_axis)), row_axis, 0, 0)]
    all_gather x1 -> x0, waiting for transfers between devices: 74.5 us -> none  [on_device(): first_weights = lax.all_gather(first_cols, 'seq', axis=0, tiled=True)]
    all_gather x1, waiting for transfers between devices: 41.1 us -> 0.01 us  [on_device(): whole = lax.all_gather(tokens, 'tp', axis=1, tiled=True)]
    ppermute x7, waiting for transfers between devices: 77.4 us -> 52.3 us  [passed_along(): return lax.ppermute(value, axis, pairs)]
    ppermute x7, starting transfers between devices: 38.7 us -> 57.8 us  [passed_along(): return lax.ppermute(value, axis, pairs)]
    all_to_all x0 -> x1, starting transfers between devices: none -> 12.1 us  [on_device(): lax.all_to_all(jnp.stack([point] * lax.axis_size(row_axis)), row_axis, 0, 0)]
    all_gather x1, waiting for transfers between devices: 7.9 us -> 0.02 us  [on_device(): lax.all_gather(w_output, 'seq', axis=1, tiled=True)]
  transfers between devices with their start and end apart: 12 -> 12, of which waited for: 9 -> 7; matrix products, arithmetic and copies ran while one was open for 14% -> 17% of each run, Pallas kernels for 0% -> 0%
where the time goes in v1:
time: 349 us; the launch traced here: 348 us
  waiting for transfers between devices  193 us (55%)
  starting transfers between devices  70 us (20%)
  other arithmetic  24.2 us (7%)
  matrix products  24 us (7%)
  local copies, waits for them, and re-layouts  22.9 us (7%)
  between operations  14.4 us (4%)
    all_to_all x1, waiting for transfers between devices, on_device(): lax.all_to_all(jnp.stack([point] * lax.axis_size(row_axis)), row_axis, 0, 0)  81.5 us
    reduce_scatter x1, waiting for transfers between devices, on_device(): lax.psum_scatter(jnp.concatenate([partial_out, square_rows], axis=0), 'tp...  57.9 us
    ppermute x7, starting transfers between devices, passed_along(): return lax.ppermute(value, axis, pairs)  57.8 us
    ppermute x7, waiting for transfers between devices, passed_along(): return lax.ppermute(value, axis, pairs)  52.3 us
    all_to_all x1, starting transfers between devices, on_device(): lax.all_to_all(jnp.stack([point] * lax.axis_size(row_axis)), row_axis, 0, 0)  12.1 us
    dot_general x1, matrix products, on_device(): jnp.dot(whole, first_weights, preferred_element_type=jnp.float32)  7.82 us
    reshape x2, local copies, waits for them, and re-layouts, on_device(): (y_inner + y_carry).reshape(row_count, inner_here)  7.59 us
  transfers between devices with their start and end apart: 12, of which 7 were waited for; matrix products, arithmetic and copies ran while one was open for 17% of the time, Pallas kernels for 0%

profile of v1, /device:TPU:1, one launch (start us, length us, event | category | flops | bytes accessed | tf_op | source)
XLA Modules:
  0.0 348.1 jit_solution(10061974807545702585)
XLA Ops:
  12.5 12.1 %all-to-all-start = ((bf16[32,64,776]{2,1,0:T(8,128)(2,1)}), bf16[32,64,776]{2,1,0:T(8,128)(2,1)}, u32[]{:S(2)}, u32[]{:S(2)}) async-start(bf16[32,64,776]{2,1,0:T(8,128)(2,1)} %stack.10), calls=%async_computation | async-start | bytes 7340032 | tf_op jit(solution)/shard_map/all_to_all | solution.py:68
  27.1 81.5 %all-to-all-done = bf16[32,64,776]{2,1,0:T(8,128)(2,1)} async-done(((bf16[32,64,776]{2,1,0:T(8,128)(2,1)}), bf16[32,64,776]{2,1,0:T(8,128)(2,1)}, u32[]{:S(2)}, u32[]{:S(2)}) %all-to-all-start) | async-done | bytes 3178528 | tf_op jit(solution)/shard_map/all_to_all | solution.py:68
  108.6 7.8 %convert_bitcast_fusion = bf16[1024,776]{1,0:T(8,128)(2,1)S(1)} fusion(bf16[2048,776]{1,0:T(8,128)(2,1)} %bitcast.1, bf16[1024,2048]{1,0:T(8,128)(2,1)} %all-gather.5.cloned.1.call-done), kind=kOutput, calls=%fused_computation.36 | convolution fusion | flops 3255574528 | bytes 8962048 | tf_op jit(solution)/shard_map/dot_general | solution.py:72
  116.5 3.9 %collective-permute-start.1 = (bf16[3,256]{1,0:T(4,128)(2,1)S(1)}, bf16[3,256]{1,0:T(4,128)(2,1)S(1)}, u32[]{:S(2)}, u32[]{:S(2)}) collective-permute-start(bf16[3,256]{1,0:T(4,128)(2,1)S(1)} %slice.235), channel_id=1, source_target_pairs={{0,8},{8,16},{16,24},{24,32},{32,40},{40,48},{48,56},{56,64},{64,7... | collective-permute-start | bytes 4616 | tf_op jit(solution)/shard_map/ppermute | solution.py:13
  120.4 4.0 %collective-permute-start = (bf16[3,512]{1,0:T(4,128)(2,1)S(1)}, bf16[3,512]{1,0:T(4,128)(2,1)S(1)}, u32[]{:S(2)}, u32[]{:S(2)}) collective-permute-start(bf16[3,512]{1,0:T(4,128)(2,1)S(1)} %slice.226), channel_id=1, source_target_pairs={{0,8},{8,16},{16,24},{24,32},{32,40},{40,48},{48,56},{56,64},{64,7... | collective-permute-start | bytes 9224 | tf_op jit(solution)/shard_map/ppermute | solution.py:13
  128.4 2.4 broadcast_multiply_fusion.3
  139.8 2.8 fusion.11
  142.9 4.6 %collective-permute-start.2 = (f32[8,129,64]{1,2,0:T(8,128)S(1)}, f32[8,129,64]{1,2,0:T(8,128)}, u32[]{:S(2)}, u32[]{:S(2)}) collective-permute-start(f32[8,129,64]{1,2,0:T(8,128)S(1)} %pad_maximum_fusion.1), channel_id=1, source_target_pairs={{0,8},{8,16},{16,24},{24,32},{32,40},{40,48},{48,56},{56,64},{64,7... | collective-permute-start | bytes 792584 | tf_op jit(solution)/shard_map/ppermute | solution.py:13
  147.4 9.2 %collective-permute-done.2 = f32[8,129,64]{1,2,0:T(8,128)} collective-permute-done((f32[8,129,64]{1,2,0:T(8,128)S(1)}, f32[8,129,64]{1,2,0:T(8,128)}, u32[]{:S(2)}, u32[]{:S(2)}) %collective-permute-start.2) | collective-permute-done | bytes 264224 | tf_op jit(solution)/shard_map/ppermute | solution.py:13
  156.6 4.2 %collective-permute-start.3 = (f32[8,129,64]{1,2,0:T(8,128)}, f32[8,129,64]{1,2,0:T(8,128)S(1)}, u32[]{:S(2)}, u32[]{:S(2)}) collective-permute-start(f32[8,129,64]{1,2,0:T(8,128)} %collective-permute-done.2), channel_id=1, source_target_pairs={{0,8},{8,16},{16,24},{24,32},{32,40},{40,48},{48,56},{56,64},{64,7... | collective-permute-start | bytes 792584 | tf_op jit(solution)/shard_map/ppermute | solution.py:13
  163.4 6.8 %collective-permute-done.3 = f32[8,129,64]{1,2,0:T(8,128)S(1)} collective-permute-done((f32[8,129,64]{1,2,0:T(8,128)}, f32[8,129,64]{1,2,0:T(8,128)S(1)}, u32[]{:S(2)}, u32[]{:S(2)}) %collective-permute-start.3) | collective-permute-done | bytes 264224 | tf_op jit(solution)/shard_map/ppermute | solution.py:13
  173.3 4.3 %collective-permute-start.4 = (f32[8,129,64]{1,2,0:T(8,128)S(1)}, f32[8,129,64]{1,2,0:T(8,128)S(1)}, u32[]{:S(2)}, u32[]{:S(2)}) collective-permute-start(f32[8,129,64]{1,2,0:T(8,128)S(1)} %pad_maximum_fusion.2), channel_id=1, source_target_pairs={{0,16},{8,24},{16,32},{24,40},{32,48},{40,56},{48,64},{56,72},{64,... | collective-permute-start | bytes 792584 | tf_op jit(solution)/shard_map/ppermute | solution.py:13
  177.8 15.7 %collective-permute-done.4 = f32[8,129,64]{1,2,0:T(8,128)S(1)} collective-permute-done((f32[8,129,64]{1,2,0:T(8,128)S(1)}, f32[8,129,64]{1,2,0:T(8,128)S(1)}, u32[]{:S(2)}, u32[]{:S(2)}) %collective-permute-start.4) | collective-permute-done | bytes 264224 | tf_op jit(solution)/shard_map/ppermute | solution.py:13
  193.8 8.2 %collective-permute-start.5 = (f32[8,129,64]{1,2,0:T(8,128)S(1)}, f32[8,129,64]{1,2,0:T(8,128)S(1)}, u32[]{:S(2)}, u32[]{:S(2)}) collective-permute-start(f32[8,129,64]{1,2,0:T(8,128)S(1)} %pad_maximum_fusion.3), channel_id=1, source_target_pairs={{0,32},{8,40},{16,48},{24,56},{32,64},{40,72},{48,80},{56,88},{64,... | collective-permute-start | bytes 792584 | tf_op jit(solution)/shard_map/ppermute | solution.py:13
  202.5 6.9 %collective-permute-done.5 = f32[8,129,64]{1,2,0:T(8,128)S(1)} collective-permute-done((f32[8,129,64]{1,2,0:T(8,128)S(1)}, f32[8,129,64]{1,2,0:T(8,128)S(1)}, u32[]{:S(2)}, u32[]{:S(2)}) %collective-permute-start.5) | collective-permute-done | bytes 264224 | tf_op jit(solution)/shard_map/ppermute | solution.py:13
  209.6 28.6 %collective-permute-start.6 = (f32[8,129,64]{1,2,0:T(8,128)S(1)}, f32[8,129,64]{1,2,0:T(8,128)S(1)}, u32[]{:S(2)}, u32[]{:S(2)}) collective-permute-start(f32[8,129,64]{1,2,0:T(8,128)S(1)} %pad_maximum_fusion.4), channel_id=1, source_target_pairs={{0,64},{8,72},{16,80},{24,88},{32,96},{40,104},{48,112},{56,120},{... | collective-permute-start | bytes 792584 | tf_op jit(solution)/shard_map/ppermute | solution.py:13
  240.4 13.7 %collective-permute-done.6 = f32[8,129,64]{1,2,0:T(8,128)S(1)} collective-permute-done((f32[8,129,64]{1,2,0:T(8,128)S(1)}, f32[8,129,64]{1,2,0:T(8,128)S(1)}, u32[]{:S(2)}, u32[]{:S(2)}) %collective-permute-start.6) | collective-permute-done | bytes 264224 | tf_op jit(solution)/shard_map/ppermute | solution.py:13
  255.4 2.4 bitcast_add_fusion
  257.8 2.8 copy.104
  260.6 4.8 %reshape.178 = f32[1024,512]{1,0:T(8,128)} reshape(f32[4,256,8,64]{3,2,1,0:T(8,128)} %copy.104) | data formatting | bytes 4194304 | tf_op jit(solution)/shard_map/reshape | solution.py:139
  265.4 6.3 %multiply_reduce_fusion = (f32[1024]{0:T(1024)S(1)}, f32[1024,512]{1,0:T(8,128)S(1)}) fusion(bf16[1024,2048]{1,0:T(8,128)(2,1)} %all-gather.5.cloned.1.call-done, bf16[2048,1,512]{2,0,1:T(8,128)(2,1)} %all-gather.9.cloned.1.call-done, f32[1024,512]{1,0:T(8,128)} %reshape.178, bf16[1024,512]{1,0:T(8,128)(2,1)S(1)} %multiply_convert_fusion.5, f32[512]{0:T(512)S(1)} %mul.490), kind=kOutput, calls=%fused_computation.31 | convolution fusion | flops 2153774080 | bytes 11540480 | tf_op jit(solution)/shard_map/dot_general | solution.py:77
  271.8 4.0 %fusion.28 = f32[1024,2048]{1,0:T(8,128)S(1)} fusion(bf16[512,2048]{0,1:T(8,128)(2,1)} %all-gather.7.cloned.1.call-done, f32[1024,512]{1,0:T(8,128)S(1)} %get-tuple-element.41, f32[512]{0:T(512)S(1)} %copy-done.4), kind=kOutput, calls=%fused_computation.40 | convolution fusion | flops 2148532224 | bytes 12584960 | tf_op jit(solution)/shard_map/dot_general | solution.py:145
  275.8 3.9 %pad_maximum_fusion = f32[1028,2048]{1,0:T(8,128)} fusion(f32[4,2048]{1,0:T(4,128)S(1)} %bitcast.120, f32[1024,2048]{1,0:T(8,128)S(1)} %fusion.28), kind=kLoop, calls=%fused_computation | loop fusion | flops 2105344 | bytes 16842752 | tf_op jit(solution)/shard_map/concatenate | solution.py:154
  280.6 57.9 %reduce-scatter.2.cloned.1.call-done = f32[1028,256]{1,0:T(8,128)} async-done(((f32[1028,2048]{1,0:T(8,128)}), f32[1028,256]{1,0:T(8,128)}) %reduce-scatter.2.cloned.1.call-update) | async-done | bytes 1052688 | tf_op jit(solution)/shard_map/reduce_scatter | solution.py:153
  (134 shorter events, 34.9 us)
Async XLA Ops:
  6.5 102.1 %all-gather.5.cloned.1.call-start = ((), (), s32[]{:S(2)}) async-start(), calls=%async_computation.2 | async-start | bytes 4718592 | tf_op jit(solution)/shard_map/all_gather | solution.py:65
  12.5 12.9 %copy-start.14 = (s32[128]{0:T(128)S(1)}, s32[128]{0:T(128)}, u32[]{:S(2)}) copy-start(s32[128]{0:T(128)} %param.24) | copy-start | bytes 1540
  12.5 13.8 %copy-start.13 = (f32[8]{0:T(128)S(1)}, f32[8]{0:T(128)}, u32[]{:S(2)}) copy-start(f32[8]{0:T(128)} %param.19) | copy-start | bytes 100
  12.5 14.6 %copy-start.6 = (f32[4,256]{1,0:T(4,128)S(1)}, f32[4,256]{1,0:T(4,128)}, u32[]{:S(2)}) copy-start(f32[4,256]{1,0:T(4,128)} %param.18) | copy-start | bytes 12292
  12.5 14.6 %copy-start.5 = (f32[4,512]{1,0:T(4,128)S(1)}, f32[4,512]{1,0:T(4,128)}, u32[]{:S(2)}) copy-start(f32[4,512]{1,0:T(4,128)} %param.17) | copy-start | bytes 24580
  12.5 96.2 %all-to-all-start = ((bf16[32,64,776]{2,1,0:T(8,128)(2,1)}), bf16[32,64,776]{2,1,0:T(8,128)(2,1)}, u32[]{:S(2)}, u32[]{:S(2)}) async-start(bf16[32,64,776]{2,1,0:T(8,128)(2,1)} %stack.10), calls=%async_computation | async-start | bytes 7340032 | tf_op jit(solution)/shard_map/all_to_all | solution.py:68
  24.6 240.8 %all-gather.9.cloned.1.call-start = ((), (), s32[]{:S(2)}) async-start(), calls=%async_computation.5 | async-start | bytes 2162688 | tf_op jit(solution)/shard_map/all_gather | solution.py:71
  25.3 246.5 %all-gather.7.cloned.1.call-start = ((), (), s32[]{:S(2)}) async-start(), calls=%async_computation.3 | async-start | bytes 2162688 | tf_op jit(solution)/shard_map/all_gather | solution.py:147
  108.6 15.8 %copy-start.11 = (f32[8]{0:T(128)S(1)}, f32[8]{0:T(128)}, u32[]{:S(2)}) copy-start(f32[8]{0:T(128)} %param.20) | copy-start | bytes 100
  116.5 14.5 %copy-start.1 = (bf16[1024,776]{1,0:T(8,128)(2,1)}, bf16[1024,776]{1,0:T(8,128)(2,1)S(1)}, u32[]{:S(2)}) copy-start(bf16[1024,776]{1,0:T(8,128)(2,1)S(1)} %convert_bitcast_fusion) | copy-start | bytes 4767748
  116.5 14.5 %collective-permute-start.1 = (bf16[3,256]{1,0:T(4,128)(2,1)S(1)}, bf16[3,256]{1,0:T(4,128)(2,1)S(1)}, u32[]{:S(2)}, u32[]{:S(2)}) collective-permute-start(bf16[3,256]{1,0:T(4,128)(2,1)S(1)} %slice.235), channel_id=1, source_target_pairs={{0,8},{8,16},{16,24},{24,32},{32,40},{40,48},{48,56},{56,64},{64,7... | collective-permute-start | bytes 4616 | tf_op jit(solution)/shard_map/ppermute | solution.py:13
  120.4 13.8 %collective-permute-start = (bf16[3,512]{1,0:T(4,128)(2,1)S(1)}, bf16[3,512]{1,0:T(4,128)(2,1)S(1)}, u32[]{:S(2)}, u32[]{:S(2)}) collective-permute-start(bf16[3,512]{1,0:T(4,128)(2,1)S(1)} %slice.226), channel_id=1, source_target_pairs={{0,8},{8,16},{16,24},{24,32},{32,40},{40,48},{48,56},{56,64},{64,7... | collective-permute-start | bytes 9224 | tf_op jit(solution)/shard_map/ppermute | solution.py:13
  142.5 19.8 %copy-start.12 = (f32[8]{0:T(128)S(1)}, f32[8]{0:T(128)}, u32[]{:S(2)}) copy-start(f32[8]{0:T(128)} %param.21) | copy-start | bytes 100
  142.7 34.9 %copy-start.8 = (f32[1,8]{1,0:T(1,128)S(1)}, f32[1,8]{1,0:T(1,128)}, u32[]{:S(2)}) copy-start(f32[1,8]{1,0:T(1,128)} %get-tuple-element.24) | copy-start | bytes 100
  142.7 34.9 %copy-start.9 = (f32[1,8]{1,0:T(1,128)S(1)}, f32[1,8]{1,0:T(1,128)}, u32[]{:S(2)}) copy-start(f32[1,8]{1,0:T(1,128)} %get-tuple-element.28) | copy-start | bytes 100
  142.7 34.9 %copy-start.10 = (f32[1,8]{1,0:T(1,128)S(1)}, f32[1,8]{1,0:T(1,128)}, u32[]{:S(2)}) copy-start(f32[1,8]{1,0:T(1,128)} %get-tuple-element.29) | copy-start | bytes 100
  142.9 13.8 %collective-permute-start.2 = (f32[8,129,64]{1,2,0:T(8,128)S(1)}, f32[8,129,64]{1,2,0:T(8,128)}, u32[]{:S(2)}, u32[]{:S(2)}) collective-permute-start(f32[8,129,64]{1,2,0:T(8,128)S(1)} %pad_maximum_fusion.1), channel_id=1, source_target_pairs={{0,8},{8,16},{16,24},{24,32},{32,40},{40,48},{48,56},{56,64},{64,7... | collective-permute-start | bytes 792584 | tf_op jit(solution)/shard_map/ppermute | solution.py:13
  156.6 13.6 %collective-permute-start.3 = (f32[8,129,64]{1,2,0:T(8,128)}, f32[8,129,64]{1,2,0:T(8,128)S(1)}, u32[]{:S(2)}, u32[]{:S(2)}) collective-permute-start(f32[8,129,64]{1,2,0:T(8,128)} %collective-permute-done.2), channel_id=1, source_target_pairs={{0,8},{8,16},{16,24},{24,32},{32,40},{40,48},{48,56},{56,64},{64,7... | collective-permute-start | bytes 792584 | tf_op jit(solution)/shard_map/ppermute | solution.py:13
  160.9 177.6 %reduce-scatter.2.cloned.1.call-start = ((), (), s32[]{:S(2)}) async-start(), calls=%async_computation.4 | async-start | bytes 9510912 | tf_op jit(solution)/shard_map/reduce_scatter | solution.py:153
  172.1 29.9 %copy-start.2 = (bf16[1024,128]{1,0:T(8,128)(2,1)S(1)}, bf16[1024,128]{1,0:T(8,128)(2,1)}, u32[]{:S(2)}) copy-start(bf16[1024,128]{1,0:T(8,128)(2,1)} %get-tuple-element.13) | copy-start | bytes 786436
  173.3 20.3 %collective-permute-start.4 = (f32[8,129,64]{1,2,0:T(8,128)S(1)}, f32[8,129,64]{1,2,0:T(8,128)S(1)}, u32[]{:S(2)}, u32[]{:S(2)}) collective-permute-start(f32[8,129,64]{1,2,0:T(8,128)S(1)} %pad_maximum_fusion.2), channel_id=1, source_target_pairs={{0,16},{8,24},{16,32},{24,40},{32,48},{40,56},{48,64},{56,72},{64,... | collective-permute-start | bytes 792584 | tf_op jit(solution)/shard_map/ppermute | solution.py:13
  193.8 15.6 %collective-permute-start.5 = (f32[8,129,64]{1,2,0:T(8,128)S(1)}, f32[8,129,64]{1,2,0:T(8,128)S(1)}, u32[]{:S(2)}, u32[]{:S(2)}) collective-permute-start(f32[8,129,64]{1,2,0:T(8,128)S(1)} %pad_maximum_fusion.3), channel_id=1, source_target_pairs={{0,32},{8,40},{16,48},{24,56},{32,64},{40,72},{48,80},{56,88},{64,... | collective-permute-start | bytes 792584 | tf_op jit(solution)/shard_map/ppermute | solution.py:13
  209.6 44.4 %collective-permute-start.6 = (f32[8,129,64]{1,2,0:T(8,128)S(1)}, f32[8,129,64]{1,2,0:T(8,128)S(1)}, u32[]{:S(2)}, u32[]{:S(2)}) collective-permute-start(f32[8,129,64]{1,2,0:T(8,128)S(1)} %pad_maximum_fusion.4), channel_id=1, source_target_pairs={{0,64},{8,72},{16,80},{24,88},{32,96},{40,104},{48,112},{56,120},{... | collective-permute-start | bytes 792584 | tf_op jit(solution)/shard_map/ppermute | solution.py:13
  265.4 6.4 %copy-start.4 = (f32[512]{0:T(512)S(1)}, f32[512]{0:T(512)}, u32[]{:S(2)}) copy-start(f32[512]{0:T(512)} %param.22) | copy-start | bytes 6148
  (8 other events, 9.2 us)
Sparse Core Ops, SparseCore 0:
  9.2 42.2 all-gather.4
  54.1 82.0 all-gather.8
  161.0 100.1 all-gather.6
  279.8 58.6 reduce-scatter.1
